TPU v7x, 128 devices: a whole 4x4x4 slice. The times are simulated.
128 devices in a mesh: page: 8 (over z, core), tensor: 16 (over x, y).
Axes of the slice: x: 4, y: 4, z: 4, core: 2. Of those that a mesh axis runs over, the one named last changes fastest.
Arguments:
- hidden_in: bfloat16 [1, 32, 8192], P(None, 'tensor', 'page'), may hold values from -6 to 6
- w_query: bfloat16 [8192, 8192], P('page', 'tensor'), may hold values from -0.0625 to 0.0625
- w_keyval: bfloat16 [8192, 2048], P('page', 'tensor'), may hold values from -0.0625 to 0.0625
- w_output: bfloat16 [8192, 8192], P('tensor', 'page'), may hold values from -0.0625 to 0.0625
- kv_pool: bfloat16 [8192, 64, 2048], P(('page', 'tensor'))
- page_table: int32 [8192], replicated, may hold values from 0 to 8191, each once
- selected: int32 [1, 32, 8, 32], replicated, may hold values from 0 to 255, as said below
Outputs:
- attn_out: bfloat16 [1, 32, 8192], P(None, 'tensor', 'page')
- new_kv: bfloat16 [1, 32, 2048], P(None, 'page', 'tensor')
Inputs may be any that keep to these rules, and one draw needn't show every extreme that they name: `page_table`: each pool slot holds exactly one page: entry s * 256 + l is the slot of page l of sequence s. `selected`: the 32 pages of one row are different.
All inputs are finite; a program needn't handle non-finite values.
Results may differ from a plain program's by a relative error of at most 0.018.
The roundings to bfloat16 on the way count: a program that leaves them out, or rounds other values in their place, can miss the bound.
Values may be sent and summed in bfloat16 or wider, within the bound.
No kernel may reach another device: no remote copies, remote signals or barrier semaphores. Data moves between devices by JAX's collectives and lax.ppermute only.
A program may use at most 192 MiB of HBM per device.

v0:
```python
import math
import jax
import jax.numpy as jnp
from jax import lax
from jax.sharding import PartitionSpec as P

H = 64
KVH = 8
HD = 128
PAGE_TOK = 64
PAGES = 256
NEG_BIG = -1e30


def frequencies(head_dim):
    half_dim = head_dim // 2
    index = jnp.arange(half_dim, dtype=jnp.float32)
    base_freq = jnp.exp(-(2.0 * index / head_dim) * math.log(500000.0))
    wavelen = 2.0 * math.pi / base_freq
    smooth = (8192.0 / wavelen - 1.0) / 3.0
    middle = (1.0 - smooth) * base_freq / 8.0 + smooth * base_freq
    scaled = jnp.where(wavelen > 8192.0, base_freq / 8.0, base_freq)
    is_middle = jnp.logical_and(wavelen >= 2048.0, wavelen <= 8192.0)
    return jnp.where(is_middle, middle, scaled)


def rotate(vectors, position):
    half_dim = vectors.shape[-1] // 2
    angles = position * frequencies(vectors.shape[-1])
    cosine = jnp.cos(angles)
    sine_v = jnp.sin(angles)
    first_half = vectors[..., :half_dim]
    second_half = vectors[..., half_dim:]
    return jnp.concatenate(
        [first_half * cosine - second_half * sine_v, first_half * sine_v + second_half * cosine],
        axis=-1,
    )


def finish(summed, position, query_cols, kind_ids):
    n_rows = summed.shape[0]
    query = rotate(summed[:, :query_cols].reshape(n_rows, query_cols // HD, HD), position)
    query = query.reshape(n_rows, query_cols).astype(jnp.bfloat16)
    keyval = summed[:, query_cols:].reshape(n_rows, -1, HD)
    rotated = rotate(keyval, position)
    keyval = jnp.where(kind_ids[None, :, None] == 0, rotated, keyval)
    return (query, keyval.reshape(n_rows, -1).astype(jnp.bfloat16))


def per_device(hidden_in, w_query, w_keyval, w_output, kv_pool, page_table, selected):
    n_page = lax.axis_size("page")
    n_tensor = lax.axis_size("tensor")
    my_page = lax.axis_index("page")
    my_tensor = lax.axis_index("tensor")
    seqs = selected.shape[1]
    groups = H // KVH
    local_heads = H // n_tensor
    scale = 1.0 / math.sqrt(HD)
    slots = kv_pool.shape[0]
    pool_size = page_table.shape[0]
    device = my_page * n_tensor + my_tensor
    logical = (
        jnp.zeros((pool_size,), jnp.int32)
        .at[page_table]
        .set(jnp.arange(pool_size, dtype=jnp.int32))
    )
    my_logical = lax.dynamic_slice_in_dim(logical, device * slots, slots)
    seq_of = my_logical // PAGES
    page_of = my_logical % PAGES
    owner_rows = jnp.arange(seqs, dtype=jnp.int32)[:, None] == seq_of[None, :]
    owner_hot = owner_rows.astype(jnp.float32)
    w_joined = jnp.concatenate([w_query, w_keyval], axis=1)
    query_cols = w_query.shape[1]
    sub_heads = w_keyval.shape[1] // HD
    kind_ids = (my_tensor * sub_heads + jnp.arange(sub_heads, dtype=jnp.int32)) % 2
    pool_five = kv_pool.reshape(slots, PAGE_TOK, KVH, 2, HD)
    key_rows = pool_five[:, :, :, 0]
    val_rows = pool_five[:, :, :, 1]
    seq_share = seqs // n_page
    position = float(PAGES * PAGE_TOK)
    tok_rows = hidden_in[0]
    partial_value = jnp.dot(
        lax.all_gather(tok_rows, "tensor", axis=0, tiled=True),
        w_joined,
        preferred_element_type=jnp.float32,
    )
    summed = lax.psum(partial_value, "page")
    query, new_local = finish(summed, position, query_cols, kind_ids)
    new_rows = [lax.dynamic_slice_in_dim(new_local, my_page * seq_share, seq_share, 0)]
    query_full = lax.all_gather(query, "tensor", axis=1, tiled=True)
    sel_rows = selected[0][seq_of]
    picked = jnp.any(sel_rows == page_of[:, None, None], axis=2)
    slot_query = query_full[seq_of].reshape(slots, KVH, groups, HD)
    scores = (
        jnp.einsum("sghd,stgd->sght", slot_query, key_rows, preferred_element_type=jnp.float32)
        * scale
    )
    page_max = jnp.max(scores, axis=-1)
    weights = jnp.exp(scores - page_max[..., None]).astype(jnp.bfloat16)
    pick_mask = picked.astype(jnp.float32)[:, :, None]
    page_total = jnp.sum(weights.astype(jnp.float32), axis=-1) * pick_mask
    weighted = (
        jnp.einsum("sght,stgd->sghd", weights, val_rows, preferred_element_type=jnp.float32)
        * pick_mask[..., None]
    )
    page_max = jnp.where(picked[:, :, None], page_max, NEG_BIG)
    seq_max = jnp.max(jnp.where(owner_rows[:, :, None, None], page_max[None], NEG_BIG), axis=1)
    factor = jnp.exp(page_max - seq_max[seq_of])
    seq_total = jnp.dot(
        owner_hot, (page_total * factor).reshape(slots, H), precision=lax.Precision.HIGHEST
    )
    seq_acc = jnp.dot(
        owner_hot,
        (weighted * factor[..., None]).reshape(slots, H * HD),
        precision=lax.Precision.HIGHEST,
    ).reshape(seqs, H, HD)
    seq_max = seq_max.reshape(seqs, H)
    top_max = lax.pmax(seq_max, ("page", "tensor"))
    rescale = jnp.exp(seq_max - top_max)
    full_total, full_acc = lax.psum(
        (seq_total * rescale, seq_acc * rescale[..., None]), ("page", "tensor")
    )
    head_start = my_tensor * local_heads
    mine_total = lax.dynamic_slice_in_dim(full_total, head_start, local_heads, 1)
    mine_acc = lax.dynamic_slice_in_dim(full_acc, head_start, local_heads, 1)
    heads = (mine_acc / mine_total[..., None]).astype(jnp.bfloat16).reshape(seqs, local_heads * HD)
    outputs = [
        lax.psum_scatter(
            jnp.dot(heads, w_output, preferred_element_type=jnp.float32),
            "tensor",
            scatter_dimension=0,
            tiled=True,
        ).astype(jnp.bfloat16)
    ]
    return (jnp.stack(outputs), jnp.stack(new_rows))


def solution(mesh):
    return jax.shard_map(
        per_device,
        mesh=mesh,
        in_specs=(
            P(None, "tensor", "page"),
            P("page", "tensor"),
            P("page", "tensor"),
            P("tensor", "page"),
            P(("page", "tensor"), None, None),
            P(),
            P(),
        ),
        out_specs=(P(None, "tensor", "page"), P(None, "page", "tensor")),
        check_vma=False,
    )
```

profile of v0, /device:TPU:0, one launch (start us, length us, event | category | flops | bytes accessed | tf_op | source)
XLA Modules:
  0.0 482.4 jit_solution(10256855988019674995)
XLA Ops:
  7.2 0.8 copy.29
  8.0 24.1 %all-gather = bf16[1,32,1024]{2,0,1:T(2,128)(2,1)S(1)} all-gather(bf16[1,2,1024]{2,0,1:T(2,128)(2,1)S(1)} %copy.29), channel_id=2, replica_groups=mesh['page'=8,'tensor'=16] {'tensor'}, dimensions={1}, use_global_device_ids=true | all-gather | bytes 69632 | tf_op jit(solution)/shard_map/all_gather | solution.py:83
  32.1 2.3 fusion.12
  34.5 30.5 %scatter_custom_fusion = s32[8192]{0:T(1024)S(1)} fusion(s32[8192]{0:T(1024)S(1)} %compare_select_fusion, s32[8192]{0:T(1024)S(1)} %iota.30, s32[]{:T(128)} %constant.80.clone.1), kind=kCustom, calls=%fused_computation.46 | custom fusion | bytes 32772 | tf_op jit(solution)/shard_map/scatter | solution.py:65
  65.2 27.4 %reshape.97 = bf16[64,64,8,2,128]{4,3,2,1,0:T(2,128)(2,1)} reshape(bf16[64,64,2048]{2,1,0:T(8,128)(2,1)} %param.11) | data formatting | bytes 33554432 | tf_op jit(solution)/shard_map/reshape | solution.py:76
  92.6 33.7 %fusion.37 = (bf16[64,64,8,1,128]{4,3,2,1,0:T(2,128)(2,1)}, bf16[64,64,8,1,128]{4,3,2,1,0:T(2,128)(2,1)}) fusion(bf16[64,64,8,2,128]{4,3,2,1,0:T(2,128)(2,1)} %reshape.97), kind=kLoop, calls=%fused_computation.74 | loop fusion | bytes 33554432 | tf_op jit(solution)/shard_map/slice | solution.py:78
  126.3 0.6 gather_fusion.1
  126.9 1.3 compare_reduce_fusion
  128.3 0.6 convert_element_type.33
  130.1 0.8 slice.38
  131.2 23.4 %all_gather.7 = bf16[32,8192]{1,0:T(8,128)(2,1)S(1)} all-gather(bf16[32,512]{1,0:T(8,128)(2,1)S(1)} %bitcast.76), channel_id=1, replica_groups=mesh['page'=8,'tensor'=16] {'tensor'}, dimensions={1}, use_global_device_ids=true | all-gather | bytes 557056 | tf_op jit(solution)/shard_map/all_gather | solution.py:90
  154.6 1.2 gather_fusion
  156.1 10.3 %multiply_reduce_fusion = (f32[64,8,8]{2,1,0:T(8,128)S(1)}, f32[64,8,8,64]{3,2,1,0:T(8,128)S(1)}) fusion(bf16[64,8,8,128]{3,2,1,0:T(8,128)(2,1)S(1)} %bitcast.70, bf16[64,64,8,1,128]{4,3,2,1,0:T(2,128)(2,1)} %get-tuple-element.9), kind=kOutput, calls=%fused_computation.15 | convolution fusion | flops 67629056 | bytes 10502144 | tf_op jit(solution)/shard_map/sghd,stgd->sght/dot_general | solution.py:95
  166.4 0.8 broadcast_select_fusion
  167.3 1.7 copy.32
  168.9 1.1 select_reduce_fusion
  170.0 0.7 copy.34
  170.8 1.4 gather_fusion.2
  172.2 2.0 convert_reduce_fusion
  174.2 64.2 %pmax.7 = f32[32,64]{0,1:T(8,128)S(1)} all-reduce(f32[32,64]{0,1:T(8,128)S(1)} %bitcast.74), channel_id=1, replica_groups=mesh['page'=8,'tensor'=16] {'page','tensor'}, use_global_device_ids=true, to_apply=%region_5.6 | all-reduce | flops 2048 | bytes 16384 | tf_op jit(solution)/shard_map/pmax | solution.py:118
  238.4 2.0 multiply_multiply_fusion.1
  240.4 1.1 copy.35
  241.5 9.7 %multiply_multiply_fusion = f32[64,8,8,128]{3,2,1,0:T(8,128)S(1)} fusion(bf16[64,64,8,1,128]{4,3,2,1,0:T(2,128)(2,1)} %get-tuple-element.8, f32[64,8,8]{2,1,0:T(8,128)} %get-tuple-element.3, f32[64,8]{1,0:T(8,128)S(1)} %copy-done.3, f32[64,8,8,64]{3,2,1,0:T(8,128)S(1)} %get-tuple-element.15, f32[64,8,8]{2,1,0:T(8,128)S(1)} %get-tuple-element.14), kind=kOutput, calls=%fused_computation.13 | convolution fusion | flops 68943872 | bytes 11569152 | tf_op jit(solution)/shard_map/sght,stgd->sghd/dot_general | solution.py:103
  251.4 3.2 fusion.5
  254.6 0.7 slice_bitcast_fusion
  255.3 0.7 slice.43
  256.0 65.0 %psum.23 = f32[32,64]{0,1:T(8,128)S(1)} all-reduce(f32[32,64]{0,1:T(8,128)S(1)} %convolution_multiply_fusion), channel_id=1, replica_groups=mesh['page'=8,'tensor'=16] {'page','tensor'}, use_global_device_ids=true, to_apply=%region_8.9 | all-reduce | flops 2048 | bytes 16384 | tf_op jit(solution)/shard_map/psum | solution.py:120
  321.1 0.6 fusion.31
  321.8 78.1 %all-reduce.7.cloned.1.call-done = f32[32,64,128]{2,0,1:T(8,128)} async-done(((f32[32,64,128]{2,0,1:T(8,128)}), f32[32,64,128]{2,0,1:T(8,128)}) %all-reduce.7.cloned.1.call-update) | async-done | bytes 1048592 | tf_op jit(solution)/shard_map/psum | solution.py:120
  399.9 1.2 fusion.17
  401.0 73.9 %all-reduce.8 = bf16[32,1024]{1,0:T(8,128)(2,1)S(1)} all-reduce(f32[32,1024]{1,0:T(8,128)S(1)} %fusion.17), channel_id=3, replica_groups=mesh['page'=8,'tensor'=16] {'tensor'}, use_global_device_ids=true, to_apply=%region_9.10.clone | all-reduce | flops 32768 | bytes 196608
  475.0 0.6 fusion.27
  (44 shorter events, 1.8 us)
Async XLA Ops:
  7.2 392.7 %copy-start = (bf16[512,1024]{1,0:T(8,128)(2,1)S(1)}, bf16[512,1024]{1,0:T(8,128)(2,1)}, u32[]{:S(2)}) copy-start(bf16[512,1024]{1,0:T(8,128)(2,1)} %param.10) | copy-start | bytes 3145732
  7.2 27.3 %copy-start.4 = (s32[8192]{0:T(1024)S(1)}, s32[8192]{0:T(1024)}, u32[]{:S(2)}) copy-start(s32[8192]{0:T(1024)} %param.12) | copy-start | bytes 98308
  7.2 122.9 %all-reduce.5.cloned.1.call-start = ((), (), s32[]{:S(2)}) async-start(), calls=%async_computation | async-start | bytes 163840 | tf_op jit(solution)/shard_map/psum | solution.py:87
  34.4 365.4 %all-reduce.7.cloned.1.call-start = ((), (), s32[]{:S(2)}) async-start(), calls=%async_computation.1 | async-start | bytes 2097152 | tf_op jit(solution)/shard_map/psum | solution.py:120
  65.2 89.4 %copy-start.5 = (s32[1024]{0:T(1024)}, s32[1024]{0:T(1024)S(1)}, u32[]{:S(2)}) copy-start(s32[1024]{0:T(1024)S(1)} %pad_clamp_fusion) | copy-start | bytes 12292
  92.6 33.7 %copy-start.1 = (s32[1,32,8,32]{3,2,1,0:T(8,128)S(1)}, s32[1,32,8,32]{3,2,1,0:T(8,128)}, u32[]{:S(2)}) copy-start(s32[1,32,8,32]{3,2,1,0:T(8,128)} %param.13) | copy-start | bytes 98308
  92.6 36.3 %copy-start.10 = (u32[128]{0:T(128)S(1)}, u32[128]{0:T(128)}, u32[]{:S(2)}) copy-start(u32[128]{0:T(128)} %constant.117) | copy-start | bytes 1540
  128.2 27.6 %copy-start.6 = (f32[64]{0:T(128)}, f32[64]{0:T(128)S(1)}, u32[]{:S(2)}) copy-start(f32[64]{0:T(128)S(1)} %get-tuple-element.16) | copy-start | bytes 772
  128.2 27.6 %copy-start.8 = (f32[64]{0:T(128)}, f32[64]{0:T(128)S(1)}, u32[]{:S(2)}) copy-start(f32[64]{0:T(128)S(1)} %get-tuple-element.17) | copy-start | bytes 772
  172.2 2.0 copy-start.2
  172.2 66.2 %copy-start.3 = (f32[64,8]{1,0:T(8,128)S(1)}, f32[64,8]{1,0:T(8,128)}, u32[]{:S(2)}) copy-start(f32[64,8]{1,0:T(8,128)} %convert_element_type.33) | copy-start | bytes 6148
  251.4 69.6 %copy-start.7 = (f32[64]{0:T(128)S(1)}, f32[64]{0:T(128)}, u32[]{:S(2)}) copy-start(f32[64]{0:T(128)} %copy-done.6) | copy-start | bytes 772
  251.4 69.6 %copy-start.9 = (f32[64]{0:T(128)S(1)}, f32[64]{0:T(128)}, u32[]{:S(2)}) copy-start(f32[64]{0:T(128)} %copy-done.8) | copy-start | bytes 772
Sparse Core Ops, SparseCore 0:
  34.5 55.7 all-reduce.4
  254.7 145.0 all-reduce.6
where the time goes:
time: 484 us; the launch traced here: 482 us
  blocking collectives  251 us (52%)
  local copies, waits for them, and re-layouts  103 us (21%)
  waiting for transfers between devices  78.1 us (16%)
  matrix products  26.8 us (6%)
  between operations  15 us (3%)
  other arithmetic  9.03 us (2%)
    psum x1, waiting for transfers between devices, per_device(): lax.psum((seq_total * rescale, seq_acc * rescale[..., None]), ('page', 't...  78.1 us
    unnamed x1, blocking collectives  73.9 us
    psum x1, blocking collectives, per_device(): lax.psum((seq_total * rescale, seq_acc * rescale[..., None]), ('page', 't...  65 us
    pmax x1, blocking collectives, per_device(): top_max = lax.pmax(seq_max, ('page', 'tensor'))  64.2 us
    slice x1, local copies, waits for them, and re-layouts, per_device(): val_rows = pool_five[:, :, :, 1]  33.7 us
    scatter x1, local copies, waits for them, and re-layouts, per_device(): logical = jnp.zeros((pool_size,), jnp.int32).at[page_table].set(jnp.arang...  30.5 us
    reshape x1, local copies, waits for them, and re-layouts, per_device(): pool_five = kv_pool.reshape(slots, PAGE_TOK, KVH, 2, HD)  27.4 us
    all_gather x1, blocking collectives, per_device(): lax.all_gather(tok_rows, 'tensor', axis=0, tiled=True)  24.1 us
  transfers between devices with their start and end apart: 2, of which 1 were waited for; matrix products, arithmetic and copies ran while one was open for 20% of the time, Pallas kernels for 0%

commit v1 on v0

--- a/solution.py
+++ b/solution.py
@@ -10,6 +10,28 @@
 PAGE_TOK = 64
 PAGES = 256
 NEG_BIG = -1e30
+
+
+def laid_out(blocks, dim):
+    lengths = list(blocks.shape[1:])
+    lengths[dim] *= blocks.shape[0]
+    return jnp.moveaxis(blocks, 0, dim).reshape(lengths)
+
+
+def gather_around(x, axis, dim):
+    size = lax.axis_size(axis)
+    pairs = [(i, (i + 1) % size) for i in range(size)]
+    back = [(b, a) for a, b in pairs]
+    lower, upper = ([], [])
+    for turn in range(size - 1):
+        if turn % 2 == 0:
+            lower.append(lax.ppermute(lower[-1] if lower else x, axis, pairs))
+        else:
+            upper.append(lax.ppermute(upper[-1] if upper else x, axis, back))
+    blocks = jnp.stack([*lower[::-1], x, *upper])
+    shift = lax.axis_index(axis) - len(lower)
+    blocks = blocks[(jnp.arange(size) - shift) % size]
+    return laid_out(blocks, dim)
 
 
 def frequencies(head_dim):
@@ -87,7 +109,7 @@
     summed = lax.psum(partial_value, "page")
     query, new_local = finish(summed, position, query_cols, kind_ids)
     new_rows = [lax.dynamic_slice_in_dim(new_local, my_page * seq_share, seq_share, 0)]
-    query_full = lax.all_gather(query, "tensor", axis=1, tiled=True)
+    query_full = gather_around(query, "tensor", 1)
     sel_rows = selected[0][seq_of]
     picked = jnp.any(sel_rows == page_of[:, None, None], axis=2)
     slot_query = query_full[seq_of].reshape(slots, KVH, groups, HD)

time: 484 us -> 518 us (1.070)
  starting transfers between devices: 0.08 us -> 39.6 us
  blocking collectives: 251 us -> 230 us
  waiting for transfers between devices: 78.1 us -> 93.2 us
    ppermute x0 -> x15, starting transfers between devices: none -> 39.5 us  [the longest x7 38.2 us: gather_around(): upper.append(lax.ppermute(upper[-1] if upper else x, axis, back))]
    all_gather x1 -> x0, blocking collectives: 23.4 us -> none  [per_device(): query_full = lax.all_gather(query, 'tensor', axis=1, tiled=True)]
    ppermute x0 -> x15, waiting for transfers between devices: none -> 14.6 us  [the longest x8 11.3 us: gather_around(): lower.append(lax.ppermute(lower[-1] if lower else x, axis, pairs))]
  transfers between devices with their start and end apart: 2 -> 17, of which waited for: 1 -> 10; matrix products, arithmetic and copies ran while one was open for 20% -> 19% of each run, Pallas kernels for 0% -> 0%
where the time goes in v1:
time: 518 us; the launch traced here: 516 us
  blocking collectives  230 us (44%)
  local copies, waits for them, and re-layouts  103 us (20%)
  waiting for transfers between devices  93.2 us (18%)
  starting transfers between devices  39.6 us (8%)
  matrix products  26.7 us (5%)
  between operations  15.2 us (3%)
  other arithmetic  9.6 us (2%)
    psum x1, waiting for transfers between devices, per_device(): lax.psum((seq_total * rescale, seq_acc * rescale[..., None]), ('page', 't...  78.5 us
    unnamed x1, blocking collectives  73.9 us
    pmax x1, blocking collectives, per_device(): top_max = lax.pmax(seq_max, ('page', 'tensor'))  66.4 us
    psum x1, blocking collectives, per_device(): lax.psum((seq_total * rescale, seq_acc * rescale[..., None]), ('page', 't...  65.2 us
    ppermute x7, starting transfers between devices, gather_around(): upper.append(lax.ppermute(upper[-1] if upper else x, axis, back))  38.2 us
    slice x1, local copies, waits for them, and re-layouts, per_device(): val_rows = pool_five[:, :, :, 1]  33.6 us
    scatter x1, local copies, waits for them, and re-layouts, per_device(): logical = jnp.zeros((pool_size,), jnp.int32).at[page_table].set(jnp.arang...  30.5 us
    reshape x1, local copies, waits for them, and re-layouts, per_device(): pool_five = kv_pool.reshape(slots, PAGE_TOK, KVH, 2, HD)  27.4 us
  transfers between devices with their start and end apart: 17, of which 10 were waited for; matrix products, arithmetic and copies ran while one was open for 19% of the time, Pallas kernels for 0%

profile of v1, /device:TPU:0, one launch (start us, length us, event | category | flops | bytes accessed | tf_op | source)
XLA Modules:
  0.0 516.4 jit_solution(14443161250811185182)
XLA Ops:
  8.0 24.1 %all-gather = bf16[1,32,1024]{2,0,1:T(2,128)(2,1)S(1)} all-gather(bf16[1,2,1024]{2,0,1:T(2,128)(2,1)S(1)} %copy.38), channel_id=2, replica_groups=mesh['page'=8,'tensor'=16] {'tensor'}, dimensions={1}, use_global_device_ids=true | all-gather | bytes 69632 | tf_op jit(solution)/shard_map/all_gather | solution.py:105
  32.1 2.3 fusion.12
  34.5 27.4 %reshape.161 = bf16[64,64,8,2,128]{4,3,2,1,0:T(2,128)(2,1)} reshape(bf16[64,64,2048]{2,1,0:T(8,128)(2,1)} %param.11) | data formatting | bytes 33554432 | tf_op jit(solution)/shard_map/reshape | solution.py:98
  61.9 33.6 %fusion.39 = (bf16[64,64,8,1,128]{4,3,2,1,0:T(2,128)(2,1)}, bf16[64,64,8,1,128]{4,3,2,1,0:T(2,128)(2,1)}) fusion(bf16[64,64,8,2,128]{4,3,2,1,0:T(2,128)(2,1)} %reshape.161), kind=kLoop, calls=%fused_computation.98 | loop fusion | bytes 33554432 | tf_op jit(solution)/shard_map/slice | solution.py:100
  95.5 30.5 %scatter_custom_fusion = s32[8192]{0:T(1024)S(1)} fusion(s32[8192]{0:T(1024)S(1)} %compare_select_fusion, s32[8192]{0:T(1024)S(1)} %iota.34, s32[]{:T(128)} %constant.95.clone.1), kind=kCustom, calls=%fused_computation.63 | custom fusion | bytes 32772 | tf_op jit(solution)/shard_map/scatter | solution.py:87
  127.1 1.3 collective-permute-start
  128.5 6.0 %collective-permute-done = bf16[32,512]{1,0:T(8,128)(2,1)S(1)} collective-permute-done((bf16[32,512]{1,0:T(8,128)(2,1)S(1)}, bf16[32,512]{1,0:T(8,128)(2,1)S(1)}, u32[]{:S(2)}, u32[]{:S(2)}) %collective-permute-start) | collective-permute-done | bytes 32800 | tf_op jit(solution)/shard_map/ppermute | solution.py:28
  134.6 5.4 %collective-permute-start.8 = (bf16[32,512]{1,0:T(8,128)(2,1)S(1)}, bf16[32,512]{1,0:T(8,128)(2,1)S(1)}, u32[]{:S(2)}, u32[]{:S(2)}) collective-permute-start(bf16[32,512]{1,0:T(8,128)(2,1)S(1)} %bitcast.114), channel_id=1, source_target_pairs={{1,0},{2,1},{3,2},{4,3},{5,4},{6,5},{7,6},{8,7},{9,8},{10,9},{11,1... | collective-permute-start | bytes 98312 | tf_op jit(solution)/shard_map/ppermute | solution.py:30
  140.0 1.7 collective-permute-done.1
  142.4 5.3 %collective-permute-start.9 = (bf16[32,512]{1,0:T(8,128)(2,1)S(1)}, bf16[32,512]{1,0:T(8,128)(2,1)S(1)}, u32[]{:S(2)}, u32[]{:S(2)}) collective-permute-start(bf16[32,512]{1,0:T(8,128)(2,1)S(1)} %collective-permute-done.8), channel_id=1, source_target_pairs={{1,0},{2,1},{3,2},{4,3},{5,4},{6,5},{7,6},{8,7},{9,8},{10,9},{11,1... | collective-permute-start | bytes 98312 | tf_op jit(solution)/shard_map/ppermute | solution.py:30
  147.7 1.3 collective-permute-done.2
  149.7 5.4 %collective-permute-start.10 = (bf16[32,512]{1,0:T(8,128)(2,1)S(1)}, bf16[32,512]{1,0:T(8,128)(2,1)S(1)}, u32[]{:S(2)}, u32[]{:S(2)}) collective-permute-start(bf16[32,512]{1,0:T(8,128)(2,1)S(1)} %collective-permute-done.9), channel_id=1, source_target_pairs={{1,0},{2,1},{3,2},{4,3},{5,4},{6,5},{7,6},{8,7},{9,8},{10,9},{11,1... | collective-permute-start | bytes 98312 | tf_op jit(solution)/shard_map/ppermute | solution.py:30
  155.1 1.1 collective-permute-done.3
  156.2 1.3 compare_reduce_fusion
  157.5 5.4 %collective-permute-start.11 = (bf16[32,512]{1,0:T(8,128)(2,1)S(1)}, bf16[32,512]{1,0:T(8,128)(2,1)S(1)}, u32[]{:S(2)}, u32[]{:S(2)}) collective-permute-start(bf16[32,512]{1,0:T(8,128)(2,1)S(1)} %collective-permute-done.10), channel_id=1, source_target_pairs={{1,0},{2,1},{3,2},{4,3},{5,4},{6,5},{7,6},{8,7},{9,8},{10,9},{11,1... | collective-permute-start | bytes 98312 | tf_op jit(solution)/shard_map/ppermute | solution.py:30
  164.5 5.6 %collective-permute-start.12 = (bf16[32,512]{1,0:T(8,128)(2,1)S(1)}, bf16[32,512]{1,0:T(8,128)(2,1)S(1)}, u32[]{:S(2)}, u32[]{:S(2)}) collective-permute-start(bf16[32,512]{1,0:T(8,128)(2,1)S(1)} %collective-permute-done.11), channel_id=1, source_target_pairs={{1,0},{2,1},{3,2},{4,3},{5,4},{6,5},{7,6},{8,7},{9,8},{10,9},{11,1... | collective-permute-start | bytes 98312 | tf_op jit(solution)/shard_map/ppermute | solution.py:30
  172.6 5.4 %collective-permute-start.13 = (bf16[32,512]{1,0:T(8,128)(2,1)S(1)}, bf16[32,512]{1,0:T(8,128)(2,1)S(1)}, u32[]{:S(2)}, u32[]{:S(2)}) collective-permute-start(bf16[32,512]{1,0:T(8,128)(2,1)S(1)} %collective-permute-done.12), channel_id=1, source_target_pairs={{1,0},{2,1},{3,2},{4,3},{5,4},{6,5},{7,6},{8,7},{9,8},{10,9},{11,1... | collective-permute-start | bytes 98312 | tf_op jit(solution)/shard_map/ppermute | solution.py:30
  179.6 5.6 %collective-permute-start.14 = (bf16[32,512]{1,0:T(8,128)(2,1)S(1)}, bf16[32,512]{1,0:T(8,128)(2,1)S(1)}, u32[]{:S(2)}, u32[]{:S(2)}) collective-permute-start(bf16[32,512]{1,0:T(8,128)(2,1)S(1)} %collective-permute-done.13), channel_id=1, source_target_pairs={{1,0},{2,1},{3,2},{4,3},{5,4},{6,5},{7,6},{8,7},{9,8},{10,9},{11,1... | collective-permute-start | bytes 98312 | tf_op jit(solution)/shard_map/ppermute | solution.py:30
  185.4 1.4 collective-permute-done.14
  187.4 1.2 gather_fusion.1
  188.9 10.3 %multiply_reduce_fusion = (f32[64,8,8]{2,1,0:T(8,128)S(1)}, f32[64,8,8,64]{3,2,1,0:T(8,128)S(1)}) fusion(bf16[64,8,8,128]{3,2,1,0:T(8,128)(2,1)S(1)} %bitcast.106, bf16[64,64,8,1,128]{4,3,2,1,0:T(2,128)(2,1)} %get-tuple-element.9), kind=kOutput, calls=%fused_computation.16 | convolution fusion | flops 67629056 | bytes 10502144 | tf_op jit(solution)/shard_map/sghd,stgd->sght/dot_general | solution.py:117
  200.1 1.7 copy.42
  203.6 1.4 gather_fusion.3
  205.0 2.0 convert_reduce_fusion
  207.1 66.4 %pmax.7 = f32[32,64]{0,1:T(8,128)S(1)} all-reduce(f32[32,64]{0,1:T(8,128)S(1)} %bitcast.111), channel_id=1, replica_groups=mesh['page'=8,'tensor'=16] {'page','tensor'}, use_global_device_ids=true, to_apply=%region_5.6 | all-reduce | flops 2048 | bytes 16384 | tf_op jit(solution)/shard_map/pmax | solution.py:140
  273.5 2.0 multiply_multiply_fusion.1
  275.5 9.7 %multiply_multiply_fusion = f32[64,8,8,128]{3,2,1,0:T(8,128)S(1)} fusion(bf16[64,64,8,1,128]{4,3,2,1,0:T(2,128)(2,1)} %get-tuple-element.8, f32[64,8,8]{2,1,0:T(8,128)S(1)} %get-tuple-element.3, f32[64,8]{1,0:T(8,128)} %convert_element_type.47, f32[64,8,8,64]{3,2,1,0:T(8,128)S(1)} %get-tuple-element.15, f32[64,8,8]{2,1,0:T(8,128)S(1)} %get-tuple-element.14), kind=kOutput, calls=%fused_computation.14 | convolution fusion | flops 68943872 | bytes 11569152 | tf_op jit(solution)/shard_map/sght,stgd->sghd/dot_general | solution.py:125
  285.2 3.1 fusion.5
  290.1 65.2 %psum.23 = f32[32,64]{0,1:T(8,128)S(1)} all-reduce(f32[32,64]{0,1:T(8,128)S(1)} %convolution_multiply_fusion), channel_id=1, replica_groups=mesh['page'=8,'tensor'=16] {'page','tensor'}, use_global_device_ids=true, to_apply=%region_8.9 | all-reduce | flops 2048 | bytes 16384 | tf_op jit(solution)/shard_map/psum | solution.py:142
  355.3 78.5 %all-reduce.7.cloned.1.call-done = f32[32,64,128]{2,0,1:T(8,128)} async-done(((f32[32,64,128]{2,0,1:T(8,128)}), f32[32,64,128]{2,0,1:T(8,128)}) %all-reduce.7.cloned.1.call-update) | async-done | bytes 1048592 | tf_op jit(solution)/shard_map/psum | solution.py:142
  433.9 1.2 fusion.17
  435.0 73.9 %all-reduce.8 = bf16[32,1024]{1,0:T(8,128)(2,1)S(1)} all-reduce(f32[32,1024]{1,0:T(8,128)S(1)} %fusion.17), channel_id=3, replica_groups=mesh['page'=8,'tensor'=16] {'tensor'}, use_global_device_ids=true, to_apply=%region_9.10.clone | all-reduce | flops 32768 | bytes 196608
  (102 shorter events, 14.4 us)
Async XLA Ops:
  7.2 426.7 %copy-start = (bf16[512,1024]{1,0:T(8,128)(2,1)S(1)}, bf16[512,1024]{1,0:T(8,128)(2,1)}, u32[]{:S(2)}) copy-start(bf16[512,1024]{1,0:T(8,128)(2,1)} %param.10) | copy-start | bytes 3145732
  7.2 27.3 %copy-start.6 = (s32[8192]{0:T(1024)S(1)}, s32[8192]{0:T(1024)}, u32[]{:S(2)}) copy-start(s32[8192]{0:T(1024)} %param.12) | copy-start | bytes 98308
  7.2 118.8 %all-reduce.5.cloned.1.call-start = ((), (), s32[]{:S(2)}) async-start(), calls=%async_computation | async-start | bytes 163840 | tf_op jit(solution)/shard_map/psum | solution.py:109
  34.4 399.5 %all-reduce.7.cloned.1.call-start = ((), (), s32[]{:S(2)}) async-start(), calls=%async_computation.1 | async-start | bytes 2097152 | tf_op jit(solution)/shard_map/psum | solution.py:142
  61.9 87.2 %copy-start.2 = (s32[1,32,8,32]{3,2,1,0:T(8,128)S(1)}, s32[1,32,8,32]{3,2,1,0:T(8,128)}, u32[]{:S(2)}) copy-start(s32[1,32,8,32]{3,2,1,0:T(8,128)} %param.13) | copy-start | bytes 98308
  61.9 109.5 %copy-start.14 = (u32[128]{0:T(128)S(1)}, u32[128]{0:T(128)}, u32[]{:S(2)}) copy-start(u32[128]{0:T(128)} %constant.134) | copy-start | bytes 1540
  95.5 39.0 %copy-start.10 = (f32[64]{0:T(128)}, f32[64]{0:T(128)S(1)}, u32[]{:S(2)}) copy-start(f32[64]{0:T(128)S(1)} %get-tuple-element.16) | copy-start | bytes 772
  95.5 53.5 %copy-start.12 = (f32[64]{0:T(128)}, f32[64]{0:T(128)S(1)}, u32[]{:S(2)}) copy-start(f32[64]{0:T(128)S(1)} %get-tuple-element.17) | copy-start | bytes 772
  127.1 7.4 %collective-permute-start = (bf16[32,512]{1,0:T(8,128)(2,1)S(1)}, bf16[32,512]{1,0:T(8,128)(2,1)S(1)}, u32[]{:S(2)}, u32[]{:S(2)}) collective-permute-start(bf16[32,512]{1,0:T(8,128)(2,1)S(1)} %bitcast.113), channel_id=1, source_target_pairs={{0,1},{1,2},{2,3},{3,4},{4,5},{5,6},{6,7},{7,8},{8,9},{9,10},{10,1... | collective-permute-start | bytes 98312 | tf_op jit(solution)/shard_map/ppermute | solution.py:28
  134.5 7.2 %collective-permute-start.1 = (bf16[32,512]{1,0:T(8,128)(2,1)S(1)}, bf16[32,512]{1,0:T(8,128)(2,1)S(1)}, u32[]{:S(2)}, u32[]{:S(2)}) collective-permute-start(bf16[32,512]{1,0:T(8,128)(2,1)S(1)} %collective-permute-done), channel_id=1, source_target_pairs={{0,1},{1,2},{2,3},{3,4},{4,5},{5,6},{6,7},{7,8},{8,9},{9,10},{10,1... | collective-permute-start | bytes 98312 | tf_op jit(solution)/shard_map/ppermute | solution.py:28
  134.6 14.4 %copy-start.7 = (s32[64]{0:T(128)}, s32[64]{0:T(128)S(1)}, u32[]{:S(2)}) copy-start(s32[64]{0:T(128)S(1)} %get-tuple-element.7) | copy-start | bytes 772
  134.6 7.8 %collective-permute-start.8 = (bf16[32,512]{1,0:T(8,128)(2,1)S(1)}, bf16[32,512]{1,0:T(8,128)(2,1)S(1)}, u32[]{:S(2)}, u32[]{:S(2)}) collective-permute-start(bf16[32,512]{1,0:T(8,128)(2,1)S(1)} %bitcast.114), channel_id=1, source_target_pairs={{1,0},{2,1},{3,2},{4,3},{5,4},{6,5},{7,6},{8,7},{9,8},{10,9},{11,1... | collective-permute-start | bytes 98312 | tf_op jit(solution)/shard_map/ppermute | solution.py:30
  141.8 7.2 %collective-permute-start.2 = (bf16[32,512]{1,0:T(8,128)(2,1)S(1)}, bf16[32,512]{1,0:T(8,128)(2,1)S(1)}, u32[]{:S(2)}, u32[]{:S(2)}) collective-permute-start(bf16[32,512]{1,0:T(8,128)(2,1)S(1)} %collective-permute-done.1), channel_id=1, source_target_pairs={{0,1},{1,2},{2,3},{3,4},{4,5},{5,6},{6,7},{7,8},{8,9},{9,10},{10,1... | collective-permute-start | bytes 98312 | tf_op jit(solution)/shard_map/ppermute | solution.py:28
  142.4 7.3 %collective-permute-start.9 = (bf16[32,512]{1,0:T(8,128)(2,1)S(1)}, bf16[32,512]{1,0:T(8,128)(2,1)S(1)}, u32[]{:S(2)}, u32[]{:S(2)}) collective-permute-start(bf16[32,512]{1,0:T(8,128)(2,1)S(1)} %collective-permute-done.8), channel_id=1, source_target_pairs={{1,0},{2,1},{3,2},{4,3},{5,4},{6,5},{7,6},{8,7},{9,8},{10,9},{11,1... | collective-permute-start | bytes 98312 | tf_op jit(solution)/shard_map/ppermute | solution.py:30
  149.0 7.2 %collective-permute-start.3 = (bf16[32,512]{1,0:T(8,128)(2,1)S(1)}, bf16[32,512]{1,0:T(8,128)(2,1)S(1)}, u32[]{:S(2)}, u32[]{:S(2)}) collective-permute-start(bf16[32,512]{1,0:T(8,128)(2,1)S(1)} %collective-permute-done.2), channel_id=1, source_target_pairs={{0,1},{1,2},{2,3},{3,4},{4,5},{5,6},{6,7},{7,8},{8,9},{9,10},{10,1... | collective-permute-start | bytes 98312 | tf_op jit(solution)/shard_map/ppermute | solution.py:28
  149.0 39.6 %copy-start.9 = (s32[1024]{0:T(1024)}, s32[1024]{0:T(1024)S(1)}, u32[]{:S(2)}) copy-start(s32[1024]{0:T(1024)S(1)} %pad_clamp_fusion) | copy-start | bytes 12292
  149.7 7.8 %collective-permute-start.10 = (bf16[32,512]{1,0:T(8,128)(2,1)S(1)}, bf16[32,512]{1,0:T(8,128)(2,1)S(1)}, u32[]{:S(2)}, u32[]{:S(2)}) collective-permute-start(bf16[32,512]{1,0:T(8,128)(2,1)S(1)} %collective-permute-done.9), channel_id=1, source_target_pairs={{1,0},{2,1},{3,2},{4,3},{5,4},{6,5},{7,6},{8,7},{9,8},{10,9},{11,1... | collective-permute-start | bytes 98312 | tf_op jit(solution)/shard_map/ppermute | solution.py:30
  156.2 7.2 %collective-permute-start.4 = (bf16[32,512]{1,0:T(8,128)(2,1)S(1)}, bf16[32,512]{1,0:T(8,128)(2,1)S(1)}, u32[]{:S(2)}, u32[]{:S(2)}) collective-permute-start(bf16[32,512]{1,0:T(8,128)(2,1)S(1)} %collective-permute-done.3), channel_id=1, source_target_pairs={{0,1},{1,2},{2,3},{3,4},{4,5},{5,6},{6,7},{7,8},{8,9},{9,10},{10,1... | collective-permute-start | bytes 98312 | tf_op jit(solution)/shard_map/ppermute | solution.py:28
  157.5 41.8 %copy-start.4 = (pred[64,8]{1,0:T(8,128)(4,1)}, pred[64,8]{1,0:T(8,128)(4,1)S(1)}, u32[]{:S(2)}) copy-start(pred[64,8]{1,0:T(8,128)(4,1)S(1)} %compare_reduce_fusion) | copy-start | bytes 1540
  157.5 7.0 %collective-permute-start.11 = (bf16[32,512]{1,0:T(8,128)(2,1)S(1)}, bf16[32,512]{1,0:T(8,128)(2,1)S(1)}, u32[]{:S(2)}, u32[]{:S(2)}) collective-permute-start(bf16[32,512]{1,0:T(8,128)(2,1)S(1)} %collective-permute-done.10), channel_id=1, source_target_pairs={{1,0},{2,1},{3,2},{4,3},{5,4},{6,5},{7,6},{8,7},{9,8},{10,9},{11,1... | collective-permute-start | bytes 98312 | tf_op jit(solution)/shard_map/ppermute | solution.py:30
  163.5 7.2 %collective-permute-start.5 = (bf16[32,512]{1,0:T(8,128)(2,1)S(1)}, bf16[32,512]{1,0:T(8,128)(2,1)S(1)}, u32[]{:S(2)}, u32[]{:S(2)}) collective-permute-start(bf16[32,512]{1,0:T(8,128)(2,1)S(1)} %collective-permute-done.4), channel_id=1, source_target_pairs={{0,1},{1,2},{2,3},{3,4},{4,5},{5,6},{6,7},{7,8},{8,9},{9,10},{10,1... | collective-permute-start | bytes 98312 | tf_op jit(solution)/shard_map/ppermute | solution.py:28
  164.5 8.1 %collective-permute-start.12 = (bf16[32,512]{1,0:T(8,128)(2,1)S(1)}, bf16[32,512]{1,0:T(8,128)(2,1)S(1)}, u32[]{:S(2)}, u32[]{:S(2)}) collective-permute-start(bf16[32,512]{1,0:T(8,128)(2,1)S(1)} %collective-permute-done.11), channel_id=1, source_target_pairs={{1,0},{2,1},{3,2},{4,3},{5,4},{6,5},{7,6},{8,7},{9,8},{10,9},{11,1... | collective-permute-start | bytes 98312 | tf_op jit(solution)/shard_map/ppermute | solution.py:30
  170.7 7.3 %collective-permute-start.6 = (bf16[32,512]{1,0:T(8,128)(2,1)S(1)}, bf16[32,512]{1,0:T(8,128)(2,1)S(1)}, u32[]{:S(2)}, u32[]{:S(2)}) collective-permute-start(bf16[32,512]{1,0:T(8,128)(2,1)S(1)} %collective-permute-done.5), channel_id=1, source_target_pairs={{0,1},{1,2},{2,3},{3,4},{4,5},{5,6},{6,7},{7,8},{8,9},{9,10},{10,1... | collective-permute-start | bytes 98312 | tf_op jit(solution)/shard_map/ppermute | solution.py:28
  172.6 7.0 %collective-permute-start.13 = (bf16[32,512]{1,0:T(8,128)(2,1)S(1)}, bf16[32,512]{1,0:T(8,128)(2,1)S(1)}, u32[]{:S(2)}, u32[]{:S(2)}) collective-permute-start(bf16[32,512]{1,0:T(8,128)(2,1)S(1)} %collective-permute-done.12), channel_id=1, source_target_pairs={{1,0},{2,1},{3,2},{4,3},{5,4},{6,5},{7,6},{8,7},{9,8},{10,9},{11,1... | collective-permute-start | bytes 98312 | tf_op jit(solution)/shard_map/ppermute | solution.py:30
  178.0 7.2 %collective-permute-start.7 = (bf16[32,512]{1,0:T(8,128)(2,1)S(1)}, bf16[32,512]{1,0:T(8,128)(2,1)S(1)}, u32[]{:S(2)}, u32[]{:S(2)}) collective-permute-start(bf16[32,512]{1,0:T(8,128)(2,1)S(1)} %collective-permute-done.6), channel_id=1, source_target_pairs={{0,1},{1,2},{2,3},{3,4},{4,5},{5,6},{6,7},{7,8},{8,9},{9,10},{10,1... | collective-permute-start | bytes 98312 | tf_op jit(solution)/shard_map/ppermute | solution.py:28
  179.6 7.2 %collective-permute-start.14 = (bf16[32,512]{1,0:T(8,128)(2,1)S(1)}, bf16[32,512]{1,0:T(8,128)(2,1)S(1)}, u32[]{:S(2)}, u32[]{:S(2)}) collective-permute-start(bf16[32,512]{1,0:T(8,128)(2,1)S(1)} %collective-permute-done.13), channel_id=1, source_target_pairs={{1,0},{2,1},{3,2},{4,3},{5,4},{6,5},{7,6},{8,7},{9,8},{10,9},{11,1... | collective-permute-start | bytes 98312 | tf_op jit(solution)/shard_map/ppermute | solution.py:30
  205.0 2.0 copy-start.3
  205.0 68.5 %copy-start.5 = (pred[64,8]{1,0:T(8,128)(4,1)S(1)}, pred[64,8]{1,0:T(8,128)(4,1)}, u32[]{:S(2)}) copy-start(pred[64,8]{1,0:T(8,128)(4,1)} %copy-done.4) | copy-start | bytes 1540
  275.5 9.7 %copy-start.8 = (s32[64]{0:T(128)S(1)}, s32[64]{0:T(128)}, u32[]{:S(2)}) copy-start(s32[64]{0:T(128)} %copy-done.7) | copy-start | bytes 772
  285.2 3.2 copy-start.11
  285.2 3.2 copy-start.13
  285.2 4.6 copy-start.1
Sparse Core Ops, SparseCore 0:
  34.5 55.7 all-reduce.4
  288.5 145.3 all-reduce.6
